TPU v7x, 256 devices: a whole 4x4x8 slice. The times are simulated.
256 devices in a mesh: dp: 8 (over z_hi, x), seq: 32 (over y, z_lo, core).
Axes of the slice: x: 4, y: 4, z: 8 (z_hi: 2, z_lo: 4; z = z_hi * 4 + z_lo), core: 2. Of those that a mesh axis runs over, the one named last changes fastest.
Arguments:
- inputs: bfloat16 [8, 32768, 1024], P('dp', 'seq'), may hold values from -6 to 6
- cotangent: bfloat16 [8, 32768, 1024], P('dp', 'seq'), may hold values from -4 to 4
- factor_one: bfloat16 [32, 1024, 1024], P('seq'), may hold values from -0.1875 to 0.1875
- factor_two: bfloat16 [32, 1024, 1024], P('seq'), may hold values from -0.1875 to 0.1875
Outputs:
- mixed: bfloat16 [8, 32768, 1024], P('dp', 'seq')
- grad_input: bfloat16 [8, 32768, 1024], P('dp', 'seq')
- grad_one: float32 [32, 1024, 1024], P('seq', 'dp')
- grad_two: float32 [32, 1024, 1024], P('seq', 'dp')
All inputs are finite; a program needn't handle non-finite values.
Results may differ from a plain program's by a relative error of at most 0.014.
Values may be sent and summed in bfloat16 or wider, within the bound.
No kernel may reach another device: no remote copies, remote signals or barrier semaphores. Data moves between devices by JAX's collectives and lax.ppermute only.
A program may use at most 128 MiB of HBM per device.

v0:
```python
import jax
import jax.numpy as jnp
from jax import lax
from jax.sharding import PartitionSpec as P


def local(inputs, cotangent, factor_one, factor_two):
    seqs, block, width = inputs.shape
    count = lax.axis_size("seq")
    rows = block // count
    fone = factor_one[0]
    ftwo = factor_two[0]
    xfull = inputs.astype(jnp.float32)
    dyfull = cotangent.astype(jnp.float32)
    first = jnp.einsum("kj,sjc->skc", fone, inputs, preferred_element_type=jnp.float32).astype(
        jnp.bfloat16
    )
    gated = (dyfull * xfull).astype(jnp.bfloat16)
    moved = lax.all_to_all(
        first.reshape(seqs, count, rows, 1, width), "seq", split_axis=1, concat_axis=3, tiled=True
    )
    moved = moved.reshape(seqs, block, width)
    second = jnp.einsum("pq,sqc->spc", ftwo, moved, preferred_element_type=jnp.float32).astype(
        jnp.bfloat16
    )
    monarch = lax.all_to_all(
        second.reshape(seqs, 1, rows, count, width), "seq", split_axis=3, concat_axis=1, tiled=True
    )
    monarch = monarch.reshape(seqs, block, width)
    gated_moved = lax.all_to_all(
        gated.reshape(seqs, count, rows, 1, width), "seq", split_axis=1, concat_axis=3, tiled=True
    )
    gated_moved = gated_moved.reshape(seqs, block, width)
    back_two = jnp.einsum(
        "pq,spc->sqc", ftwo, gated_moved, preferred_element_type=jnp.float32
    ).astype(jnp.bfloat16)
    back_moved = lax.all_to_all(
        back_two.reshape(seqs, 1, rows, count, width),
        "seq",
        split_axis=3,
        concat_axis=1,
        tiled=True,
    )
    back_moved = back_moved.reshape(seqs, block, width)
    mfull = monarch.astype(jnp.float32)
    mixed = (xfull * mfull).astype(jnp.bfloat16)
    part_two = jnp.einsum("spc,sqc->pq", gated_moved, moved, preferred_element_type=jnp.float32)
    part_one = jnp.einsum("skc,sjc->kj", back_moved, inputs, preferred_element_type=jnp.float32)
    grad_one, grad_two = (
        lax.psum_scatter(
            part_one.astype(jnp.bfloat16), "dp", scatter_dimension=0, tiled=True
        ).astype(jnp.float32),
        lax.psum_scatter(
            part_two.astype(jnp.bfloat16), "dp", scatter_dimension=0, tiled=True
        ).astype(jnp.float32),
    )
    spread = jnp.einsum("kj,skc->sjc", fone, back_moved, preferred_element_type=jnp.float32)
    grad_input = (dyfull * mfull + spread).astype(jnp.bfloat16)
    return (mixed, grad_input, grad_one[None], grad_two[None])


def solution(mesh):
    in_specs = (
        P("dp", "seq", None),
        P("dp", "seq", None),
        P("seq", None, None),
        P("seq", None, None),
    )
    out_specs = (
        P("dp", "seq", None),
        P("dp", "seq", None),
        P("seq", "dp", None),
        P("seq", "dp", None),
    )
    return jax.shard_map(local, mesh=mesh, in_specs=in_specs, out_specs=out_specs, check_vma=False)
```

profile of v0, /device:TPU:8, one launch (start us, length us, event | category | flops | bytes accessed | tf_op | source)
XLA Modules:
  0.0 429.8 jit_solution(16111633440075535005)
XLA Ops:
  7.2 0.0 copy-start
  7.2 4.7 %fusion.17 = bf16[1024,1024]{0,1:T(8,128)(2,1)S(1)} fusion(bf16[1,1024,1024]{2,1,0:T(8,128)(2,1)} %param.4, bf16[1,1024,1024]{2,1,0:T(8,128)(2,1)} %param.6), kind=kOutput, calls=%fused_computation.19 | convolution fusion | flops 2148532224 | bytes 6291456 | tf_op jit(solution)/shard_map/kj,sjc->skc/dot_general | solution.py:15
  11.9 56.7 %all_to_all.54 = bf16[1,32,32,1,1024]{4,2,3,0,1:T(8,128)(2,1)S(1)} all-to-all(bf16[1,32,32,1,1024]{4,2,3,0,1:T(8,128)(2,1)S(1)} %bitcast.90), channel_id=1, replica_groups=mesh['dp'=8,'seq'=32] {'seq'}, dimensions={1} | all-to-all | bytes 4194304 | tf_op jit(solution)/shard_map/all_to_all | solution.py:19
  68.6 1.2 copy.26
  69.8 0.0 copy-start.1
  69.8 0.0 copy-done
  69.8 2.4 fusion.22
  72.1 0.0 copy-done.1
  72.2 2.5 copy.27
  74.6 7.2 %all-to-all-start.1 = ((bf16[1,1,32,32,1024]{4,2,1,0,3:T(8,128)(2,1)}), bf16[1,1,32,32,1024]{4,2,1,0,3:T(8,128)(2,1)}, u32[]{:S(2)}, u32[]{:S(2)}) async-start(bf16[1,1,32,32,1024]{4,2,1,0,3:T(8,128)(2,1)} %copy.27), calls=%async_computation.1 | async-start | bytes 4194304 | tf_op jit(solution)/shard_map/all_to_all | solution.py:26
  81.8 3.9 copy.24
  85.7 3.9 copy.30
  89.7 40.1 %all-to-all-done.1 = bf16[1,1,32,32,1024]{4,2,1,0,3:T(8,128)(2,1)} async-done(((bf16[1,1,32,32,1024]{4,2,1,0,3:T(8,128)(2,1)}), bf16[1,1,32,32,1024]{4,2,1,0,3:T(8,128)(2,1)}, u32[]{:S(2)}, u32[]{:S(2)}) %all-to-all-start.1) | async-done | bytes 2097184 | tf_op jit(solution)/shard_map/all_to_all | solution.py:26
  129.7 4.1 bitcast_convert_fusion
  133.8 5.3 %copy.29 = f32[1,1024,1024]{1,2,0:T(8,128)} copy(f32[1,1024,1024]{2,1,0:T(8,128)} %bitcast.84) | data formatting | bytes 8388608 | tf_op jit(solution)/shard_map/convert_element_type | solution.py:45
  139.1 6.9 %fusion.3 = (bf16[1,1024,1024]{1,2,0:T(8,128)(2,1)}, bf16[1,1024,1024]{1,2,0:T(8,128)(2,1)}) fusion(bf16[1,1024,1024]{1,2,0:T(8,128)(2,1)} %copy.24, bf16[1,1024,1024]{1,2,0:T(8,128)(2,1)} %copy.30, f32[1,1024,1024]{1,2,0:T(8,128)} %copy.29), kind=kLoop, calls=%fused_computation.6 | loop fusion | flops 6291456 | bytes 12582912 | tf_op jit(solution)/shard_map/convert_element_type | solution.py:18
  146.0 3.9 copy.32
  149.9 54.3 %all_to_all.55 = bf16[1,32,32,1,1024]{4,2,3,0,1:T(8,128)(2,1)S(1)} all-to-all(bf16[1,32,32,1,1024]{4,2,3,0,1:T(8,128)(2,1)} %bitcast.85), channel_id=1, replica_groups=mesh['dp'=8,'seq'=32] {'seq'}, dimensions={1} | all-to-all | bytes 4194304 | tf_op jit(solution)/shard_map/all_to_all | solution.py:30
  204.2 1.2 copy.34
  205.4 0.0 copy-start.2
  205.4 2.4 fusion.25
  207.8 0.0 copy-done.2
  207.9 2.5 copy.35
  210.3 7.2 %all-to-all-start.3 = ((bf16[1,1,32,32,1024]{4,2,1,0,3:T(8,128)(2,1)}), bf16[1,1,32,32,1024]{4,2,1,0,3:T(8,128)(2,1)}, u32[]{:S(2)}, u32[]{:S(2)}) async-start(bf16[1,1,32,32,1024]{4,2,1,0,3:T(8,128)(2,1)} %copy.35), calls=%async_computation.3 | async-start | bytes 4194304 | tf_op jit(solution)/shard_map/all_to_all | solution.py:37
  217.6 0.0 reduce-scatter.5.cloned.1.call-start
  217.6 5.9 %convolution_convert_fusion = bf16[1024,1024]{1,0:T(8,128)(2,1)} fusion(bf16[1024,1024]{1,0:T(8,128)(2,1)} %bitcast.89, bf16[1024,1024]{1,0:T(8,128)(2,1)} %bitcast.87), kind=kOutput, calls=%fused_computation.22 | convolution fusion | flops 2148532224 | bytes 6291456 | tf_op jit(solution)/shard_map/spc,sqc->pq/dot_general | solution.py:47
  223.5 0.0 reduce-scatter.5.cloned.1.call-update
  223.6 0.3 reduce-scatter.3.cloned.1.call-start
  223.8 59.9 %all-to-all-done.3 = bf16[1,1,32,32,1024]{4,2,1,0,3:T(8,128)(2,1)} async-done(((bf16[1,1,32,32,1024]{4,2,1,0,3:T(8,128)(2,1)}), bf16[1,1,32,32,1024]{4,2,1,0,3:T(8,128)(2,1)}, u32[]{:S(2)}, u32[]{:S(2)}) %all-to-all-start.3) | async-done | bytes 2097184 | tf_op jit(solution)/shard_map/all_to_all | solution.py:37
  283.8 5.9 %fusion.14 = bf16[1024,1024]{1,0:T(8,128)(2,1)} fusion(bf16[1024,1024]{1,0:T(8,128)(2,1)} %bitcast.29, bf16[1,1024,1024]{2,1,0:T(8,128)(2,1)} %param.4), kind=kOutput, calls=%fused_computation.18 | convolution fusion | flops 2148532224 | bytes 6291456 | tf_op jit(solution)/shard_map/skc,sjc->kj/dot_general | solution.py:48
  289.7 0.0 reduce-scatter.3.cloned.1.call-update
  289.7 3.9 copy.36
  293.7 7.9 %fusion.2 = bf16[1,1024,1024]{1,2,0:T(8,128)(2,1)} fusion(f32[1,1024,1024]{1,2,0:T(8,128)} %copy.29, bf16[1,1024,1024]{1,2,0:T(8,128)(2,1)} %copy.30, bf16[1024,1024]{1,0:T(8,128)(2,1)} %bitcast.29, bf16[1,1024,1024]{2,1,0:T(8,128)(2,1)} %param.6), kind=kOutput, calls=%fused_computation.5 | convolution fusion | flops 2151677952 | bytes 12582912 | tf_op jit(solution)/shard_map/kj,skc->sjc/dot_general | solution.py:57
  301.6 3.9 copy.37
  305.5 20.0 %reduce-scatter.5.cloned.1.call-done = bf16[128,1024]{1,0:T(8,128)(2,1)} async-done(((bf16[1024,1024]{1,0:T(8,128)(2,1)}), bf16[128,1024]{1,0:T(8,128)(2,1)}) %reduce-scatter.5.cloned.1.call-update) | async-done | bytes 262160 | tf_op jit(solution)/shard_map/reduce_scatter | solution.py:53
  325.5 1.8 bitcast_convert_fusion.1
  327.3 93.9 %reduce-scatter.3.cloned.1.call-done = bf16[128,1024]{1,0:T(8,128)(2,1)} async-done(((bf16[1024,1024]{1,0:T(8,128)(2,1)}), bf16[128,1024]{1,0:T(8,128)(2,1)}) %reduce-scatter.3.cloned.1.call-update) | async-done | bytes 262160 | tf_op jit(solution)/shard_map/reduce_scatter | solution.py:50
  421.2 1.8 bitcast_convert_fusion.2
Async XLA Ops:
  7.2 62.6 %copy-start = (bf16[1,1024,1024]{2,1,0:T(8,128)(2,1)S(1)}, bf16[1,1024,1024]{2,1,0:T(8,128)(2,1)}, u32[]{:S(2)}) copy-start(bf16[1,1024,1024]{2,1,0:T(8,128)(2,1)} %param.7) | copy-start | bytes 6291460
  69.8 2.4 copy-start.1
  74.6 55.1 %all-to-all-start.1 = ((bf16[1,1,32,32,1024]{4,2,1,0,3:T(8,128)(2,1)}), bf16[1,1,32,32,1024]{4,2,1,0,3:T(8,128)(2,1)}, u32[]{:S(2)}, u32[]{:S(2)}) async-start(bf16[1,1,32,32,1024]{4,2,1,0,3:T(8,128)(2,1)} %copy.27), calls=%async_computation.1 | async-start | bytes 4194304 | tf_op jit(solution)/shard_map/all_to_all | solution.py:26
  205.4 2.5 copy-start.2
  210.3 73.4 %all-to-all-start.3 = ((bf16[1,1,32,32,1024]{4,2,1,0,3:T(8,128)(2,1)}), bf16[1,1,32,32,1024]{4,2,1,0,3:T(8,128)(2,1)}, u32[]{:S(2)}, u32[]{:S(2)}) async-start(bf16[1,1,32,32,1024]{4,2,1,0,3:T(8,128)(2,1)} %copy.35), calls=%async_computation.3 | async-start | bytes 4194304 | tf_op jit(solution)/shard_map/all_to_all | solution.py:37
  217.6 108.0 %reduce-scatter.5.cloned.1.call-start = ((), (), s32[]{:S(2)}) async-start(), calls=%async_computation.7 | async-start | bytes 2359296 | tf_op jit(solution)/shard_map/reduce_scatter | solution.py:53
  223.6 197.6 %reduce-scatter.3.cloned.1.call-start = ((), (), s32[]{:S(2)}) async-start(), calls=%async_computation.6 | async-start | bytes 2359296 | tf_op jit(solution)/shard_map/reduce_scatter | solution.py:50
Sparse Core Ops, SparseCore 0:
  223.7 101.8 reduce-scatter.4
  329.6 91.5 reduce-scatter.2
where the time goes:
time: 431 us; the launch traced here: 430 us
  waiting for transfers between devices  214 us (50%)
  blocking collectives  111 us (26%)
  local copies, waits for them, and re-layouts  32.3 us (7%)
  matrix products  29.2 us (7%)
  starting transfers between devices  14.7 us (3%)
  other arithmetic  14.5 us (3%)
  between operations  14.1 us (3%)
    reduce_scatter x1, waiting for transfers between devices, local(): lax.psum_scatter(part_one.astype(jnp.bfloat16), 'dp', scatter_dimension=0...  93.9 us
    all_to_all x1, waiting for transfers between devices, local(): lax.all_to_all(back_two.reshape(seqs, 1, rows, count, width), 'seq', spli...  59.9 us
    all_to_all x1, blocking collectives, local(): lax.all_to_all(first.reshape(seqs, count, rows, 1, width), 'seq', split_a...  56.7 us
    all_to_all x1, blocking collectives, local(): lax.all_to_all(gated.reshape(seqs, count, rows, 1, width), 'seq', split_a...  54.3 us
    all_to_all x1, waiting for transfers between devices, local(): lax.all_to_all(second.reshape(seqs, 1, rows, count, width), 'seq', split_...  40.1 us
    reduce_scatter x1, waiting for transfers between devices, local(): lax.psum_scatter(part_two.astype(jnp.bfloat16), 'dp', scatter_dimension=0...  20 us
    unnamed x10, local copies, waits for them, and re-layouts  15.8 us
  transfers between devices with their start and end apart: 4, of which 4 were waited for; matrix products, arithmetic and copies ran while one was open for 9% of the time, Pallas kernels for 0%

commit v1 on v0

--- a/solution.py
+++ b/solution.py
@@ -27,8 +27,16 @@
         second.reshape(seqs, 1, rows, count, width), "seq", split_axis=3, concat_axis=1, tiled=True
     )
     monarch = monarch.reshape(seqs, block, width)
-    gated_moved = lax.all_to_all(
-        gated.reshape(seqs, count, rows, 1, width), "seq", split_axis=1, concat_axis=3, tiled=True
+    gated_moved = jnp.concatenate(
+        lax.all_to_all(
+            jnp.stack(
+                jnp.split(gated.reshape(seqs, count, rows, 1, width), lax.axis_size("seq"), axis=1)
+            ),
+            "seq",
+            0,
+            0,
+        ),
+        axis=3,
     )
     gated_moved = gated_moved.reshape(seqs, block, width)
     back_two = jnp.einsum(

time: 431 us -> 445 us (1.032)
  local copies, waits for them, and re-layouts: 32.3 us -> 46.1 us
    unnamed x10 -> x43, local copies, waits for them, and re-layouts: 15.8 us -> 29.5 us
  transfers between devices with their start and end apart: 4 -> 4, of which waited for: 4 -> 4; matrix products, arithmetic and copies ran while one was open for 9% -> 8% of each run, Pallas kernels for 0% -> 0%
where the time goes in v1:
time: 445 us; the launch traced here: 443 us
  waiting for transfers between devices  214 us (48%)
  blocking collectives  111 us (25%)
  local copies, waits for them, and re-layouts  46.1 us (10%)
  matrix products  29.3 us (7%)
  starting transfers between devices  14.6 us (3%)
  other arithmetic  14.5 us (3%)
  between operations  14.3 us (3%)
    reduce_scatter x1, waiting for transfers between devices, local(): lax.psum_scatter(part_one.astype(jnp.bfloat16), 'dp', scatter_dimension=0...  93.8 us
    all_to_all x1, waiting for transfers between devices, local(): lax.all_to_all(back_two.reshape(seqs, 1, rows, count, width), 'seq', spli...  59.9 us
    all_to_all x1, blocking collectives, local(): lax.all_to_all(first.reshape(seqs, count, rows, 1, width), 'seq', split_a...  56.7 us
    all_to_all x1, blocking collectives, local(): lax.all_to_all(jnp.stack(jnp.split(gated.reshape(seqs, count, rows, 1, wi...  54 us
    all_to_all x1, waiting for transfers between devices, local(): lax.all_to_all(second.reshape(seqs, 1, rows, count, width), 'seq', split_...  40.1 us
    unnamed x43, local copies, waits for them, and re-layouts  29.5 us
    reduce_scatter x1, waiting for transfers between devices, local(): lax.psum_scatter(part_two.astype(jnp.bfloat16), 'dp', scatter_dimension=0...  19.9 us
  transfers between devices with their start and end apart: 4, of which 4 were waited for; matrix products, arithmetic and copies ran while one was open for 8% of the time, Pallas kernels for 0%

profile of v1, /device:TPU:8, one launch (start us, length us, event | category | flops | bytes accessed | tf_op | source)
XLA Modules:
  0.0 443.2 jit_solution(1343551758639980163)
XLA Ops:
  7.2 4.7 %fusion.17 = bf16[1024,1024]{0,1:T(8,128)(2,1)S(1)} fusion(bf16[1,1024,1024]{2,1,0:T(8,128)(2,1)} %param.4, bf16[1,1024,1024]{2,1,0:T(8,128)(2,1)} %param.6), kind=kOutput, calls=%fused_computation.19 | convolution fusion | flops 2148532224 | bytes 6291456 | tf_op jit(solution)/shard_map/kj,sjc->skc/dot_general | solution.py:15
  11.9 56.7 %all_to_all.44 = bf16[1,32,32,1,1024]{4,2,3,0,1:T(8,128)(2,1)S(1)} all-to-all(bf16[1,32,32,1,1024]{4,2,3,0,1:T(8,128)(2,1)S(1)} %bitcast.276), channel_id=1, replica_groups=mesh['dp'=8,'seq'=32] {'seq'}, dimensions={1} | all-to-all | bytes 4194304 | tf_op jit(solution)/shard_map/all_to_all | solution.py:19
  68.6 1.2 copy.87
  69.8 2.4 fusion.22
  72.2 2.5 copy.88
  74.6 7.1 %all-to-all-start.1 = ((bf16[1,1,32,32,1024]{4,2,1,0,3:T(8,128)(2,1)}), bf16[1,1,32,32,1024]{4,2,1,0,3:T(8,128)(2,1)}, u32[]{:S(2)}, u32[]{:S(2)}) async-start(bf16[1,1,32,32,1024]{4,2,1,0,3:T(8,128)(2,1)} %copy.88), calls=%async_computation.1 | async-start | bytes 4194304 | tf_op jit(solution)/shard_map/all_to_all | solution.py:26
  81.8 3.9 copy.85
  85.7 3.9 copy.91
  89.6 40.1 %all-to-all-done.1 = bf16[1,1,32,32,1024]{4,2,1,0,3:T(8,128)(2,1)} async-done(((bf16[1,1,32,32,1024]{4,2,1,0,3:T(8,128)(2,1)}), bf16[1,1,32,32,1024]{4,2,1,0,3:T(8,128)(2,1)}, u32[]{:S(2)}, u32[]{:S(2)}) %all-to-all-start.1) | async-done | bytes 2097184 | tf_op jit(solution)/shard_map/all_to_all | solution.py:26
  129.7 4.1 bitcast_convert_fusion
  133.8 5.4 %copy.90 = f32[1,1024,1024]{1,2,0:T(8,128)} copy(f32[1,1024,1024]{2,1,0:T(8,128)} %bitcast.238) | data formatting | bytes 8388608 | tf_op jit(solution)/shard_map/convert_element_type | solution.py:53
  139.1 6.9 %fusion.3 = (bf16[1,1024,1024]{1,2,0:T(8,128)(2,1)}, bf16[1,1024,1024]{1,2,0:T(8,128)(2,1)}) fusion(bf16[1,1024,1024]{1,2,0:T(8,128)(2,1)} %copy.85, bf16[1,1024,1024]{1,2,0:T(8,128)(2,1)} %copy.91, f32[1,1024,1024]{1,2,0:T(8,128)} %copy.90), kind=kLoop, calls=%fused_computation.6 | loop fusion | flops 6291456 | bytes 12582912 | tf_op jit(solution)/shard_map/convert_element_type | solution.py:18
  146.0 3.9 copy.93
  149.9 1.0 constant_dynamic-update-slice_fusion.31
  150.9 0.8 constant_dynamic-update-slice_fusion.30
  151.8 0.8 constant_dynamic-update-slice_fusion.29
  152.6 0.8 constant_dynamic-update-slice_fusion.28
  153.5 0.8 constant_dynamic-update-slice_fusion.27
  154.3 0.8 constant_dynamic-update-slice_fusion.26
  155.1 0.8 constant_dynamic-update-slice_fusion.25
  156.0 0.8 constant_dynamic-update-slice_fusion.24
  156.8 0.8 constant_dynamic-update-slice_fusion.23
  157.7 0.8 constant_dynamic-update-slice_fusion.22
  158.5 0.8 constant_dynamic-update-slice_fusion.21
  159.4 0.8 constant_dynamic-update-slice_fusion.20
  160.2 0.8 constant_dynamic-update-slice_fusion.19
  161.1 0.8 constant_dynamic-update-slice_fusion.18
  161.9 0.8 constant_dynamic-update-slice_fusion.17
  162.7 0.8 constant_dynamic-update-slice_fusion.16
  163.8 54.0 %all_to_all.45 = bf16[32,1,1,32,1,1024]{5,3,4,2,1,0:T(8,128)(2,1)S(1)} all-to-all(bf16[32,1,1,32,1,1024]{5,3,4,2,1,0:T(8,128)(2,1)S(1)} %constant_dynamic-update-slice_fusion), channel_id=1, replica_groups=mesh['dp'=8,'seq'=32] {'seq'}, dimensions={0} | all-to-all | bytes 4194304 | tf_op jit(solution)/shard_map/all_to_all | solution.py:31
  217.9 1.2 copy.124
  219.0 2.4 fusion.25
  221.5 2.5 copy.125
  223.9 7.1 %all-to-all-start.3 = ((bf16[1,1,32,32,1024]{4,2,1,0,3:T(8,128)(2,1)}), bf16[1,1,32,32,1024]{4,2,1,0,3:T(8,128)(2,1)}, u32[]{:S(2)}, u32[]{:S(2)}) async-start(bf16[1,1,32,32,1024]{4,2,1,0,3:T(8,128)(2,1)} %copy.125), calls=%async_computation.3 | async-start | bytes 4194304 | tf_op jit(solution)/shard_map/all_to_all | solution.py:45
  231.1 0.0 reduce-scatter.5.cloned.1.call-start
  231.2 5.9 %convolution_convert_fusion = bf16[1024,1024]{1,0:T(8,128)(2,1)} fusion(bf16[1024,1024]{1,0:T(8,128)(2,1)} %bitcast.275, bf16[1024,1024]{1,0:T(8,128)(2,1)} %bitcast.273), kind=kOutput, calls=%fused_computation.22 | convolution fusion | flops 2148532224 | bytes 6291456 | tf_op jit(solution)/shard_map/spc,sqc->pq/dot_general | solution.py:55
  237.1 0.0 reduce-scatter.5.cloned.1.call-update
  237.1 0.3 reduce-scatter.3.cloned.1.call-start
  237.4 59.9 %all-to-all-done.3 = bf16[1,1,32,32,1024]{4,2,1,0,3:T(8,128)(2,1)} async-done(((bf16[1,1,32,32,1024]{4,2,1,0,3:T(8,128)(2,1)}), bf16[1,1,32,32,1024]{4,2,1,0,3:T(8,128)(2,1)}, u32[]{:S(2)}, u32[]{:S(2)}) %all-to-all-start.3) | async-done | bytes 2097184 | tf_op jit(solution)/shard_map/all_to_all | solution.py:45
  297.3 6.0 %fusion.14 = bf16[1024,1024]{1,0:T(8,128)(2,1)} fusion(bf16[1024,1024]{1,0:T(8,128)(2,1)} %bitcast.89, bf16[1,1024,1024]{2,1,0:T(8,128)(2,1)} %param.4), kind=kOutput, calls=%fused_computation.18 | convolution fusion | flops 2148532224 | bytes 6291456 | tf_op jit(solution)/shard_map/skc,sjc->kj/dot_general | solution.py:56
  303.3 0.0 reduce-scatter.3.cloned.1.call-update
  303.3 3.9 copy.126
  307.2 7.9 %fusion.2 = bf16[1,1024,1024]{1,2,0:T(8,128)(2,1)} fusion(f32[1,1024,1024]{1,2,0:T(8,128)} %copy.90, bf16[1,1024,1024]{1,2,0:T(8,128)(2,1)} %copy.91, bf16[1024,1024]{1,0:T(8,128)(2,1)} %bitcast.89, bf16[1,1024,1024]{2,1,0:T(8,128)(2,1)} %param.6), kind=kOutput, calls=%fused_computation.5 | convolution fusion | flops 2151677952 | bytes 12582912 | tf_op jit(solution)/shard_map/kj,skc->sjc/dot_general | solution.py:65
  315.1 3.9 copy.127
  319.1 19.9 %reduce-scatter.5.cloned.1.call-done = bf16[128,1024]{1,0:T(8,128)(2,1)} async-done(((bf16[1024,1024]{1,0:T(8,128)(2,1)}), bf16[128,1024]{1,0:T(8,128)(2,1)}) %reduce-scatter.5.cloned.1.call-update) | async-done | bytes 262160 | tf_op jit(solution)/shard_map/reduce_scatter | solution.py:61
  339.0 1.8 bitcast_convert_fusion.1
  340.8 93.8 %reduce-scatter.3.cloned.1.call-done = bf16[128,1024]{1,0:T(8,128)(2,1)} async-done(((bf16[1024,1024]{1,0:T(8,128)(2,1)}), bf16[128,1024]{1,0:T(8,128)(2,1)}) %reduce-scatter.3.cloned.1.call-update) | async-done | bytes 262160 | tf_op jit(solution)/shard_map/reduce_scatter | solution.py:58
  434.6 1.8 bitcast_convert_fusion.2
  (24 shorter events, 0.1 us)
Async XLA Ops:
  7.2 62.6 %copy-start = (bf16[1,1024,1024]{2,1,0:T(8,128)(2,1)S(1)}, bf16[1,1024,1024]{2,1,0:T(8,128)(2,1)}, u32[]{:S(2)}) copy-start(bf16[1,1024,1024]{2,1,0:T(8,128)(2,1)} %param.7) | copy-start | bytes 6291460
  69.8 2.4 copy-start.2
  74.6 55.1 %all-to-all-start.1 = ((bf16[1,1,32,32,1024]{4,2,1,0,3:T(8,128)(2,1)}), bf16[1,1,32,32,1024]{4,2,1,0,3:T(8,128)(2,1)}, u32[]{:S(2)}, u32[]{:S(2)}) async-start(bf16[1,1,32,32,1024]{4,2,1,0,3:T(8,128)(2,1)} %copy.88), calls=%async_computation.1 | async-start | bytes 4194304 | tf_op jit(solution)/shard_map/all_to_all | solution.py:26
  149.9 13.7 %copy-start.1 = (bf16[1,1024,1024]{2,1,0:T(8,128)(2,1)S(1)}, bf16[1,1024,1024]{2,1,0:T(8,128)(2,1)}, u32[]{:S(2)}) copy-start(bf16[1,1024,1024]{2,1,0:T(8,128)(2,1)} %copy.93) | copy-start | bytes 6291460
  219.0 2.5 copy-start.3
  223.9 73.3 %all-to-all-start.3 = ((bf16[1,1,32,32,1024]{4,2,1,0,3:T(8,128)(2,1)}), bf16[1,1,32,32,1024]{4,2,1,0,3:T(8,128)(2,1)}, u32[]{:S(2)}, u32[]{:S(2)}) async-start(bf16[1,1,32,32,1024]{4,2,1,0,3:T(8,128)(2,1)} %copy.125), calls=%async_computation.3 | async-start | bytes 4194304 | tf_op jit(solution)/shard_map/all_to_all | solution.py:45
  231.1 107.9 %reduce-scatter.5.cloned.1.call-start = ((), (), s32[]{:S(2)}) async-start(), calls=%async_computation.7 | async-start | bytes 2359296 | tf_op jit(solution)/shard_map/reduce_scatter | solution.py:61
  237.1 197.5 %reduce-scatter.3.cloned.1.call-start = ((), (), s32[]{:S(2)}) async-start(), calls=%async_computation.6 | async-start | bytes 2359296 | tf_op jit(solution)/shard_map/reduce_scatter | solution.py:58
Sparse Core Ops, SparseCore 0:
  237.2 101.7 reduce-scatter.4
  343.1 91.4 reduce-scatter.2
